TPU v7x, 32 devices: a whole 2x2x4 slice. The times are simulated.
32 devices in a mesh: dp: 8 (over y, x, core), expert: 4 (over z).
Axes of the slice: x: 2, y: 2, z: 4, core: 2. Of those that a mesh axis runs over, the one named last changes fastest.
Arguments:
- hidden: bfloat16 [2, 512, 2880], P(None, ('dp', 'expert')), may hold values from -1.5 to 1.5
- norm_gain: float32 [2880], replicated, may hold values from 0.1 to 1.9
- router: bfloat16 [2880, 64], replicated, may hold values from -0.078125 to 0.078125
- routes: int32 [2, 512, 4], P(None, ('dp', 'expert')), may hold values from 0 to 63, all different within a row; in each aligned block of 16 rows (0 to 15, 16 to 31, ..., all dimensions but the last counted through in order) at most 2 rows name the same one
- w_gate: bfloat16 [64, 2880, 2048], P('expert', None, 'dp'), may hold values from -0.109375 to 0.109375
- w_up: bfloat16 [64, 2880, 2048], P('expert', None, 'dp'), may hold values from -0.109375 to 0.109375
- w_down: bfloat16 [64, 2048, 2880], P('expert', 'dp'), may hold values from -0.125 to 0.125
- queries: bfloat16 [2, 512, 4096], P(None, ('dp', 'expert')), may hold values from -5.5 to 5.5
- new_key: bfloat16 [2, 512, 512], P(None, ('dp', 'expert')), may hold values from -8 to 8
- new_value: bfloat16 [2, 512, 512], P(None, ('dp', 'expert')), may hold values from -6 to 6
- key_pages: bfloat16 [256, 4, 16, 512], P(('dp', 'expert')), may hold values from -6 to 6
- value_pages: bfloat16 [256, 4, 16, 512], P(('dp', 'expert')), may hold values from -6 to 6
- page_counts: int32 [32, 16], P(('dp', 'expert')), may hold values from 1 to 10, 32 in all within a row
- page_order: int32 [32, 32], P(('dp', 'expert')), may hold values from 0 to 31, each once within a row
Outputs:
- context: bfloat16 [2, 512, 4096], P(None, ('dp', 'expert'))
- layer_out: bfloat16 [2, 512, 2880], P(None, ('dp', 'expert'))
Inputs may be any that keep to these rules, and one draw needn't show every extreme that they name: `routes`: in each step, the 16 rows of one aligned block name each expert at most 2 times, and some block names some expert exactly 2 times. `page_counts`: each block's counts sum to 32, and the largest count of a block is exactly 10. Each row of page_order is a permutation of 0 to 31.
All inputs are finite; a program needn't handle non-finite values.
Results may differ from a plain program's by a relative error of at most 0.0095.
Values may be sent and summed in bfloat16 or wider, within the bound.
No kernel may reach another device: no remote copies, remote signals or barrier semaphores. Data moves between devices by JAX's collectives and lax.ppermute only.
A program may use at most 192 MiB of HBM per device.

v0:
```python
import jax
import jax.numpy as jnp
from jax import lax
from jax.sharding import PartitionSpec as P

HEADS = 64
KV_HEADS = 8
HEAD_DIM = 64
EXPERTS = 64
MOST = 2
STEPS = 2
BLOCK = 16


def page_layout(counts, page_perm, most_pages):
    starts = jnp.cumsum(counts) - counts
    offsets = jnp.arange(most_pages, dtype=jnp.int32)
    places = starts[:, None] + offsets[None, :]
    places = jnp.where(offsets[None, :] < counts[:, None], places, 0)
    return jnp.take(page_perm, places, axis=0)


def attention(query_rows, fresh_keys, fresh_values, space_keys, space_values, counts, page_perm):
    group_size = HEADS // KV_HEADS
    most_pages = page_perm.shape[0] // 3
    row_count = counts.shape[0]
    cache_span = most_pages * BLOCK
    slot_ids = page_layout(counts, page_perm, most_pages).reshape(-1)
    cache_keys = jnp.take(space_keys, slot_ids, axis=0).reshape(
        row_count, cache_span, KV_HEADS, HEAD_DIM
    )
    cache_values = jnp.take(space_values, slot_ids, axis=0).reshape(
        row_count, cache_span, KV_HEADS, HEAD_DIM
    )
    live_mask = jnp.arange(cache_span)[None, :] < (counts * BLOCK)[:, None]
    query_heads = query_rows.reshape(STEPS, row_count, KV_HEADS, group_size, HEAD_DIM)
    new_keys = fresh_keys.reshape(STEPS, row_count, KV_HEADS, HEAD_DIM)
    new_values = fresh_values.reshape(STEPS, row_count, KV_HEADS, HEAD_DIM)
    score_scale = HEAD_DIM ** (-0.5)
    old_scores = (
        jnp.einsum("trkgh,rlkh->trkgl", query_heads, cache_keys, preferred_element_type=jnp.float32)
        * score_scale
    )
    old_scores = jnp.where(live_mask[None, :, None, None, :], old_scores, -jnp.inf)
    new_scores = (
        jnp.einsum("trkgh,urkh->trkgu", query_heads, new_keys, preferred_element_type=jnp.float32)
        * score_scale
    )
    causal = jnp.arange(STEPS)[None, :] <= jnp.arange(STEPS)[:, None]
    new_scores = jnp.where(causal[:, None, None, None, :], new_scores, -jnp.inf)
    row_max = jnp.maximum(jnp.max(old_scores, axis=-1), jnp.max(new_scores, axis=-1))
    old_probs = jnp.exp(old_scores - row_max[..., None])
    new_probs = jnp.exp(new_scores - row_max[..., None])
    denominator = jnp.sum(old_probs, axis=-1) + jnp.sum(new_probs, axis=-1)
    numerator = jnp.einsum(
        "trkgl,rlkh->trkgh",
        old_probs.astype(jnp.bfloat16),
        cache_values,
        preferred_element_type=jnp.float32,
    )
    numerator = numerator + jnp.einsum(
        "trkgu,urkh->trkgh",
        new_probs.astype(jnp.bfloat16),
        new_values,
        preferred_element_type=jnp.float32,
    )
    result = numerator / denominator[..., None]
    return result.reshape(STEPS, row_count, HEADS * HEAD_DIM).astype(jnp.bfloat16)


MOST = 2


def moe_layer(hidden, norm_gain, router, routes, w_gate, w_up, w_down):
    steps, rows, model_width = hidden.shape
    topk = routes.shape[-1]
    n_dp = lax.axis_size("dp")
    n_ex = lax.axis_size("expert")
    local_experts = w_gate.shape[0]
    blocks = n_dp * n_ex
    residual = hidden.astype(jnp.float32)
    scale_rows = lax.rsqrt(jnp.mean(residual * residual, axis=-1, keepdims=True) + 1e-05)
    normed = (residual * scale_rows * norm_gain).astype(jnp.bfloat16)
    logit_rows = jnp.einsum("trd,de->tre", normed, router, preferred_element_type=jnp.float32)
    chosen = jnp.take_along_axis(logit_rows, routes, axis=-1)
    spreads = chosen[..., None, :] - chosen[..., :, None]
    gate_vals = (1.0 / jnp.sum(jnp.exp(spreads), axis=-1)).astype(jnp.bfloat16)
    lanes = -(-(model_width + 2 * topk) // 128) * 128
    filler = jnp.zeros((steps, rows, lanes - model_width - 2 * topk), jnp.bfloat16)
    payload = jnp.concatenate([normed, gate_vals, routes.astype(jnp.bfloat16), filler], axis=-1)
    gathered = lax.all_gather(payload, ("dp", "expert"), axis=1, tiled=False)
    return (gathered, residual)


def moe_finish(gathered, meta, residual, topk, w_gate, w_up, w_down):
    steps, rows, model_width = residual.shape
    n_dp = lax.axis_size("dp")
    n_ex = lax.axis_size("expert")
    local_experts = w_gate.shape[0]
    all_rows = gathered[..., :model_width]
    all_gates = meta[..., :topk]
    all_ids = jnp.round(meta[..., topk : 2 * topk]).astype(jnp.int32)
    first = lax.axis_index("expert") * local_experts
    numbers = first + jnp.arange(local_experts, dtype=jnp.int32)
    matches = all_ids[..., None] == numbers
    picked = jnp.any(matches, axis=-2).astype(jnp.int32)
    gate_of = jnp.sum(jnp.where(matches, all_gates[..., None].astype(jnp.float32), 0.0), axis=-2)
    earlier = jnp.cumsum(picked, axis=2) - picked
    ranks = jnp.arange(MOST, dtype=jnp.int32)
    sender = (picked[..., None] > 0) & (earlier[..., None] == ranks)
    slots = jnp.einsum(
        "tbrxm,tbrd->tbxmd",
        sender.astype(jnp.bfloat16),
        all_rows,
        preferred_element_type=jnp.float32,
    ).astype(jnp.bfloat16)
    gate_part = jnp.einsum("tbxmd,xdf->tbxmf", slots, w_gate, preferred_element_type=jnp.float32)
    up_part = jnp.einsum("tbxmd,xdf->tbxmf", slots, w_up, preferred_element_type=jnp.float32)
    hidden_act = ((up_part + 1.0) * gate_part * jax.nn.sigmoid(1.702 * gate_part)).astype(
        jnp.bfloat16
    )
    partial = jnp.einsum(
        "tbxmf,xfd->tbxmd", hidden_act, w_down, preferred_element_type=jnp.float32
    ).astype(jnp.bfloat16)
    weights = jnp.where(sender, gate_of[..., None], 0.0).astype(jnp.bfloat16)
    grid = (steps, n_dp, n_ex)
    if local_experts * MOST < rows:
        summed = lax.psum_scatter(
            partial.astype(jnp.float32).reshape(grid + partial.shape[2:]),
            "dp",
            scatter_dimension=1,
            tiled=True,
        )[:, 0]
        own = lax.axis_index("dp")
        own_weights = lax.dynamic_index_in_dim(
            weights.reshape(grid + weights.shape[2:]), own, 1, False
        )
        row_terms = jnp.einsum(
            "terxm,texmd->terd",
            own_weights.astype(jnp.float32),
            summed,
            precision=lax.Precision.HIGHEST,
            preferred_element_type=jnp.float32,
        )
    else:
        row_terms = jnp.einsum(
            "tbrxm,tbxmd->btrd", weights, partial, preferred_element_type=jnp.float32
        ).astype(jnp.bfloat16)
        row_terms = lax.psum_scatter(
            row_terms.reshape((n_dp, n_ex) + row_terms.shape[1:]),
            "dp",
            scatter_dimension=0,
            tiled=True,
        )[0]
        shares = lax.all_to_all(row_terms, "expert", split_axis=0, concat_axis=0, tiled=True)
        branch_out = jnp.sum(shares.astype(jnp.float32), axis=0)
        return (residual + branch_out).astype(jnp.bfloat16)
    branch_out = lax.psum_scatter(row_terms, "expert", scatter_dimension=1, tiled=True)
    return (residual + branch_out[:, 0].astype(jnp.float32)).astype(jnp.bfloat16)


def body(
    hidden,
    norm_gain,
    router,
    routes,
    w_gate,
    w_up,
    w_down,
    queries,
    new_key,
    new_value,
    key_pages,
    value_pages,
    page_counts,
    page_order,
):
    host_keys, host_values = (
        lax.all_to_all(key_pages, "dp", split_axis=0, concat_axis=0, tiled=True),
        lax.all_to_all(value_pages, "dp", split_axis=0, concat_axis=0, tiled=True),
    )
    kv_width = KV_HEADS * HEAD_DIM
    space_keys = host_keys.reshape(-1, BLOCK, kv_width)
    space_values = host_values.reshape(-1, BLOCK, kv_width)
    gathered, residual = moe_layer(hidden, norm_gain, router, routes, w_gate, w_up, w_down)
    context = attention(
        queries, new_key, new_value, space_keys, space_values, page_counts[0], page_order[0]
    )
    meta = gathered[..., hidden.shape[-1] :]
    gathered, meta, context = lax.optimization_barrier((gathered, meta, context))
    layer_out = moe_finish(gathered, meta, residual, routes.shape[-1], w_gate, w_up, w_down)
    return (context, layer_out)


def solution(mesh):
    return jax.shard_map(
        body,
        mesh=mesh,
        in_specs=(
            P(None, ("dp", "expert"), None),
            P(),
            P(),
            P(None, ("dp", "expert"), None),
            P("expert", None, "dp"),
            P("expert", None, "dp"),
            P("expert", "dp", None),
            P(None, ("dp", "expert"), None),
            P(None, ("dp", "expert"), None),
            P(None, ("dp", "expert"), None),
            P(("dp", "expert"), None, None, None),
            P(("dp", "expert"), None, None, None),
            P(("dp", "expert"), None),
            P(("dp", "expert"), None),
        ),
        out_specs=(P(None, ("dp", "expert"), None), P(None, ("dp", "expert"), None)),
        check_vma=False,
    )
```

profile of v0, /device:TPU:0, one launch (start us, length us, event | category | flops | bytes accessed | tf_op | source)
XLA Modules:
  0.0 261.9 jit_solution(6205403180816961716)
XLA Ops:
  7.2 0.7 convert_element_type.73
  8.0 0.8 copy.104
  8.7 1.0 fusion.53
  10.2 1.0 fusion.55
  11.5 1.5 gather_fusion.1
  13.4 0.8 concatenate.3
  14.2 5.2 %all-to-all-start = ((bf16[8,4,16,512]{3,2,1,0:T(8,128)(2,1)}), bf16[8,4,16,512]{3,2,1,0:T(8,128)(2,1)S(1)}, u32[]{:S(2)}, u32[]{:S(2)}) async-start(bf16[8,4,16,512]{3,2,1,0:T(8,128)(2,1)} %param.27), calls=%async_computation | async-start | bytes 1048576 | tf_op jit(solution)/shard_map/all_to_all | solution.py:180
  21.1 1.6 gather_fusion
  22.7 6.6 %all-to-all-done = bf16[8,4,16,512]{3,2,1,0:T(8,128)(2,1)S(1)} async-done(((bf16[8,4,16,512]{3,2,1,0:T(8,128)(2,1)}), bf16[8,4,16,512]{3,2,1,0:T(8,128)(2,1)S(1)}, u32[]{:S(2)}, u32[]{:S(2)}) %all-to-all-start) | async-done | bytes 524320 | tf_op jit(solution)/shard_map/all_to_all | solution.py:180
  29.3 3.5 %all-to-all-start.1 = ((bf16[8,4,16,512]{3,2,1,0:T(8,128)(2,1)}), bf16[8,4,16,512]{3,2,1,0:T(8,128)(2,1)S(1)}, u32[]{:S(2)}, u32[]{:S(2)}) async-start(bf16[8,4,16,512]{3,2,1,0:T(8,128)(2,1)} %param.26), calls=%async_computation.1 | async-start | bytes 1048576 | tf_op jit(solution)/shard_map/all_to_all | solution.py:179
  32.9 3.2 %fusion.68 = (f32[2,16,8,8]{3,0,2,1:T(2,128)S(1)}, f32[2,16,8,8,2]{3,4,0,2,1:T(2,128)}) fusion(bf16[2,16,8,8,64]{4,3,2,1,0:T(8,128)(2,1)S(1)} %reshape.268, bf16[2,16,8,64,1]{3,2,1,0,4:T(8,128)(2,1)S(1)} %bitcast.102, pred[2,2]{1,0:T(4,128)(4,1)S(1)} %iota_compare_fusion.3), kind=kOutput, calls=%fused_computation.101 | convolution fusion | flops 534528 | bytes 319492 | tf_op jit(solution)/shard_map/trkgh,urkh->trkgu/dot_general | solution.py:46
  36.1 2.5 gather_fusion.2
  38.6 3.9 %all-to-all-done.1 = bf16[8,4,16,512]{3,2,1,0:T(8,128)(2,1)S(1)} async-done(((bf16[8,4,16,512]{3,2,1,0:T(8,128)(2,1)}), bf16[8,4,16,512]{3,2,1,0:T(8,128)(2,1)S(1)}, u32[]{:S(2)}, u32[]{:S(2)}) %all-to-all-start.1) | async-done | bytes 524320 | tf_op jit(solution)/shard_map/all_to_all | solution.py:179
  42.4 2.5 gather_fusion.3
  44.9 4.4 %broadcast_select_fusion = (bf16[160,16,512]{2,1,0:T(8,128)(2,1)}, bf16[160,16,512]{2,1,0:T(8,128)(2,1)S(1)}) fusion(bf16[160,16,512]{2,1,0:T(8,128)(2,1)} %gather_fusion.3, pred[160]{0:T(512)(128)(4,1)S(1)} %get-tuple-element.9, bf16[160,16,512]{2,1,0:T(8,128)(2,1)} %gather_fusion.2), kind=kLoop, calls=%fused_computation.23 | loop fusion | flops 2621440 | bytes 10485920 | tf_op jit(solution)/shard_map/jit(_take)/select_n | solution.py:29
  49.4 7.5 %reshape.267 = bf16[16,160,8,64]{3,2,1,0:T(8,128)(2,1)} reshape(bf16[160,16,512]{2,1,0:T(8,128)(2,1)} %get-tuple-element.15) | data formatting | bytes 5242880 | tf_op jit(solution)/shard_map/reshape | solution.py:29
  56.8 4.6 %reshape.265 = bf16[16,160,8,64]{3,2,1,0:T(8,128)(2,1)} reshape(bf16[160,16,512]{2,1,0:T(8,128)(2,1)S(1)} %get-tuple-element.16) | data formatting | bytes 5242880 | tf_op jit(solution)/shard_map/reshape | solution.py:32
  61.4 6.4 %bitcast_reduce_fusion = (f32[2,16,8,8]{3,0,2,1:T(2,128)S(1)}, f32[16,8,160,2,8]{2,4,3,1,0:T(8,128)S(1)}) fusion(pred[16,160]{1,0:T(8,128)(4,1)S(1)} %iota_compare_fusion.1, bf16[2,16,8,8,64]{4,3,2,1,0:T(8,128)(2,1)S(1)} %reshape.268, bf16[16,160,8,64,1]{3,2,1,0,4:T(8,128)(2,1)} %bitcast.99), kind=kOutput, calls=%fused_computation.26 | convolution fusion | flops 42924032 | bytes 4205056 | tf_op jit(solution)/shard_map/trkgh,rlkh->trkgl/dot_general | solution.py:41
  68.4 1.0 fusion.25
  69.5 1.5 fusion.27
  71.1 0.6 fusion.37
  71.8 1.2 convert_element_type.77
  73.0 12.4 %all-gather.3.cloned.1.call-done = bf16[2,512,2944]{2,1,0:T(8,128)(2,1)} async-done(((bf16[2,16,2944]{2,1,0:T(8,128)(2,1)}), bf16[2,512,2944]{2,1,0:T(8,128)(2,1)}) %all-gather.3.cloned.1.call-update) | async-done | bytes 6029328 | tf_op jit(solution)/shard_map/all_gather | solution.py:91
  85.4 1.1 slice.25
  88.9 10.5 %convolution_convert_fusion = bf16[2,32,16,2,2880]{4,2,3,1,0:T(8,128)(2,1)} fusion(bf16[2,32,16,2944]{3,2,1,0:T(8,128)(2,1)} %bitcast.93, s32[2,32,16,16]{3,2,0,1:T(8,128)S(1)} %copy.125, pred[2,32,16,16]{3,2,0,1:T(8,128)(4,1)S(1)} %copy.124), kind=kOutput, calls=%fused_computation.16 | convolution fusion | flops 194707456 | bytes 17907712 | tf_op jit(solution)/shard_map/tbrxm,tbrd->tbxmd/dot_general | solution.py:111
  99.4 13.9 %fusion.4 = f32[16,2,32,2,256]{4,2,3,1,0:T(8,128)S(1)} fusion(bf16[16,2880,256]{2,1,0:T(8,128)(2,1)} %param.21, bf16[2,32,16,2,2880]{4,2,3,1,0:T(8,128)(2,1)} %convolution_convert_fusion), kind=kOutput, calls=%fused_computation.8 | convolution fusion | flops 3019898880 | bytes 37486592 | tf_op jit(solution)/shard_map/tbxmd,xdf->tbxmf/dot_general | solution.py:118
  113.3 13.9 %fusion.32 = bf16[2,32,16,2,256]{4,1,3,0,2:T(8,128)(2,1)S(1)} fusion(bf16[16,2880,256]{2,1,0:T(8,128)(2,1)} %param.20, bf16[2,32,16,2,2880]{4,2,3,1,0:T(8,128)(2,1)} %convolution_convert_fusion, f32[16,2,32,2,256]{4,2,3,1,0:T(8,128)S(1)} %fusion.4), kind=kOutput, calls=%fused_computation.37 | convolution fusion | flops 3024093184 | bytes 38535168 | tf_op jit(solution)/shard_map/tbxmd,xdf->tbxmf/dot_general | solution.py:117
  127.3 23.1 %convert_bitcast_fusion = bf16[2,32,16,2,2880]{4,1,3,0,2:T(8,128)(2,1)} fusion(bf16[2,32,16,2,256]{4,1,3,0,2:T(8,128)(2,1)S(1)} %fusion.32, bf16[16,256,2880]{1,2,0:T(8,128)(2,1)} %param.22), kind=kOutput, calls=%fused_computation.13 | convolution fusion | flops 3025797120 | bytes 36438016 | tf_op jit(solution)/shard_map/tbxmf,xfd->tbxmd/dot_general | solution.py:122
  150.4 20.2 %bitcast_convert_fusion = bf16[32,2,16,2880]{3,2,1,0:T(8,128)(2,1)} fusion(bf16[2,32,16,2,2880]{4,1,3,0,2:T(8,128)(2,1)} %convert_bitcast_fusion, bf16[2,32,16,16]{3,2,0,1:T(8,128)(2,1)S(1)} %copy.127, s32[2,32,16,16]{3,2,0,1:T(8,128)S(1)} %copy.125, pred[2,32,16,16]{3,2,0,1:T(8,128)(4,1)S(1)} %copy.124), kind=kOutput, calls=%fused_computation.10 | convolution fusion | flops 191791104 | bytes 17809408 | tf_op jit(solution)/shard_map/tbrxm,tbxmd->btrd/dot_general | solution.py:146
  170.6 59.4 %reduce-scatter.2.cloned.1.call-done = bf16[1,4,2,16,2880]{4,3,2,1,0:T(8,128)(2,1)} async-done(((bf16[8,4,2,16,2880]{4,3,2,1,0:T(8,128)(2,1)}), bf16[1,4,2,16,2880]{4,3,2,1,0:T(8,128)(2,1)}) %reduce-scatter.2.cloned.1.call-update) | async-done | bytes 737296 | tf_op jit(solution)/shard_map/reduce_scatter | solution.py:149
  230.0 24.0 %all_to_all.15 = bf16[4,2,16,2880]{3,2,1,0:T(8,128)(2,1)S(1)} all-to-all(bf16[4,2,16,2880]{3,2,1,0:T(8,128)(2,1)} %bitcast.100), channel_id=1, replica_groups=mesh['dp'=8,'expert'=4] {'expert'}, dimensions={0} | all-to-all | bytes 1474560 | tf_op jit(solution)/shard_map/all_to_all | solution.py:155
  254.1 0.7 fusion.56
  (80 shorter events, 6.1 us)
Async XLA Ops:
  7.2 4.1 %copy-start = (bf16[2880,64]{0,1:T(8,128)(2,1)S(1)}, bf16[2880,64]{0,1:T(8,128)(2,1)}, u32[]{:S(2)}) copy-start(bf16[2880,64]{0,1:T(8,128)(2,1)} %param.18) | copy-start | bytes 1105924
  7.2 78.2 %all-gather.3.cloned.1.call-start = ((), (), s32[]{:S(2)}) async-start(), calls=%async_computation.5 | async-start | bytes 6217728 | tf_op jit(solution)/shard_map/all_gather | solution.py:91
  11.5 7.9 %copy-start.8 = (s32[1,16]{1,0:T(1,128)S(1)}, s32[1,16]{1,0:T(1,128)}, u32[]{:S(2)}) copy-start(s32[1,16]{1,0:T(1,128)} %param.28) | copy-start | bytes 196
  11.5 8.8 %copy-start.6 = (bf16[2,16,512]{2,1,0:T(8,128)(2,1)S(1)}, bf16[2,16,512]{2,1,0:T(8,128)(2,1)}, u32[]{:S(2)}) copy-start(bf16[2,16,512]{2,1,0:T(8,128)(2,1)} %param.24) | copy-start | bytes 98308
  11.5 8.9 %copy-start.7 = (bf16[2,16,512]{2,1,0:T(8,128)(2,1)S(1)}, bf16[2,16,512]{2,1,0:T(8,128)(2,1)}, u32[]{:S(2)}) copy-start(bf16[2,16,512]{2,1,0:T(8,128)(2,1)} %param.25) | copy-start | bytes 98308
  11.5 9.0 %copy-start.4 = (bf16[2,16,4096]{2,1,0:T(8,128)(2,1)S(1)}, bf16[2,16,4096]{2,1,0:T(8,128)(2,1)}, u32[]{:S(2)}) copy-start(bf16[2,16,4096]{2,1,0:T(8,128)(2,1)} %param.23) | copy-start | bytes 786436
  13.1 8.0 %copy-start.2 = (s32[1,32]{1,0:T(1,128)S(1)}, s32[1,32]{1,0:T(1,128)}, u32[]{:S(2)}) copy-start(s32[1,32]{1,0:T(1,128)} %param.29) | copy-start | bytes 388
  14.2 15.0 %all-to-all-start = ((bf16[8,4,16,512]{3,2,1,0:T(8,128)(2,1)}), bf16[8,4,16,512]{3,2,1,0:T(8,128)(2,1)S(1)}, u32[]{:S(2)}, u32[]{:S(2)}) async-start(bf16[8,4,16,512]{3,2,1,0:T(8,128)(2,1)} %param.27), calls=%async_computation | async-start | bytes 1048576 | tf_op jit(solution)/shard_map/all_to_all | solution.py:180
  29.3 13.2 %all-to-all-start.1 = ((bf16[8,4,16,512]{3,2,1,0:T(8,128)(2,1)}), bf16[8,4,16,512]{3,2,1,0:T(8,128)(2,1)S(1)}, u32[]{:S(2)}, u32[]{:S(2)}) async-start(bf16[8,4,16,512]{3,2,1,0:T(8,128)(2,1)} %param.26), calls=%async_computation.1 | async-start | bytes 1048576 | tf_op jit(solution)/shard_map/all_to_all | solution.py:179
  32.8 197.2 %reduce-scatter.2.cloned.1.call-start = ((), (), s32[]{:S(2)}) async-start(), calls=%async_computation.4 | async-start | bytes 6782976 | tf_op jit(solution)/shard_map/reduce_scatter | solution.py:149
  61.4 8.1 %slice-start = ((s8[5242880]{0:T(1024)(128)(4,1)}), s8[4194304]{0:T(1024)(128)(4,1)S(1)}, s32[]{:S(2)}) async-start(s8[5242880]{0:T(1024)(128)(4,1)} %bitcast.96), calls=%async_computation.6 | async-start | bytes 8388608
  61.4 6.4 %copy-start.5 = (f32[2,16,8,8,2]{3,4,0,2,1:T(2,128)S(1)}, f32[2,16,8,8,2]{3,4,0,2,1:T(2,128)}, u32[]{:S(2)}) copy-start(f32[2,16,8,8,2]{3,4,0,2,1:T(2,128)} %get-tuple-element.20) | copy-start | bytes 49156
  61.4 8.1 %slice-start.1 = ((s8[5242880]{0:T(1024)(128)(4,1)}), s8[1048576]{0:T(1024)(128)(4,1)S(1)}, s32[]{:S(2)}) async-start(s8[5242880]{0:T(1024)(128)(4,1)} %bitcast.96), calls=%async_computation.7 | async-start | bytes 2097152
  170.5 83.6 %copy-start.3 = (bf16[2,16,2880]{2,1,0:T(8,128)(2,1)S(1)}, bf16[2,16,2880]{2,1,0:T(8,128)(2,1)}, u32[]{:S(2)}) copy-start(bf16[2,16,2880]{2,1,0:T(8,128)(2,1)} %param.16) | copy-start | bytes 552964
  170.6 84.3 %copy-start.1 = (bf16[2880,64]{0,1:T(8,128)(2,1)S(1)}, bf16[2880,64]{0,1:T(8,128)(2,1)}, u32[]{:S(2)}) copy-start(bf16[2880,64]{0,1:T(8,128)(2,1)} %param.18) | copy-start | bytes 1105924
Sparse Core Ops, SparseCore 0:
  14.4 70.9 all-gather.2
  170.7 59.2 reduce-scatter.1
where the time goes:
time: 267 us; the launch traced here: 262 us
  matrix products  93.5 us (35%)
  waiting for transfers between devices  82.2 us (31%)
  local copies, waits for them, and re-layouts  27.8 us (10%)
  blocking collectives  24 us (9%)
  between operations  14.7 us (6%)
  other arithmetic  10.8 us (4%)
  starting transfers between devices  8.76 us (3%)
    reduce_scatter x1, waiting for transfers between devices, moe_finish(): lax.psum_scatter(row_terms.reshape((n_dp, n_ex) + row_terms.shape[1:]), '...  59.4 us
    all_to_all x1, blocking collectives, moe_finish(): lax.all_to_all(row_terms, 'expert', split_axis=0, concat_axis=0, tiled=True)  24 us
    dot_general x1, matrix products, moe_finish(): jnp.einsum('tbxmf,xfd->tbxmd', hidden_act, w_down, preferred_element_type...  23.1 us
    dot_general x1, matrix products, moe_finish(): jnp.einsum('tbrxm,tbxmd->btrd', weights, partial, preferred_element_type=...  20.2 us
    dot_general x1, matrix products, moe_finish(): jnp.einsum('tbxmd,xdf->tbxmf', slots, w_gate, preferred_element_type=jnp....  13.9 us
    dot_general x1, matrix products, moe_finish(): jnp.einsum('tbxmd,xdf->tbxmf', slots, w_up, preferred_element_type=jnp.fl...  13.9 us
    all_gather x1, waiting for transfers between devices, moe_layer(): gathered = lax.all_gather(payload, ('dp', 'expert'), axis=1, tiled=False)  12.4 us
    dot_general x1, matrix products, moe_finish(): jnp.einsum('tbrxm,tbrd->tbxmd', sender.astype(jnp.bfloat16), all_rows, pr...  10.5 us
  transfers between devices with their start and end apart: 4, of which 4 were waited for; matrix products, arithmetic and copies ran while one was open for 15% of the time, Pallas kernels for 0%

commit v1 on v0

--- a/solution.py
+++ b/solution.py
@@ -10,6 +10,22 @@
 MOST = 2
 STEPS = 2
 BLOCK = 16
+
+
+def exchange_in_pairs(x, axis, split, join):
+    ways, here = (lax.axis_size(axis), lax.axis_index(axis))
+    width = x.shape[split] // ways
+    shape = list(x.shape)
+    shape[split] = width
+    height = shape[join]
+    shape[join] = height * ways
+    full = jnp.zeros(shape, x.dtype)
+    for mask in range(ways):
+        part = lax.dynamic_slice_in_dim(x, (here ^ mask) * width, width, axis=split)
+        if mask:
+            part = lax.ppermute(part, axis, [(d, d ^ mask) for d in range(ways)])
+        full = lax.dynamic_update_slice_in_dim(full, part, (here ^ mask) * height, axis=join)
+    return full
 
 
 def page_layout(counts, page_perm, most_pages):
@@ -176,7 +192,7 @@
     page_order,
 ):
     host_keys, host_values = (
-        lax.all_to_all(key_pages, "dp", split_axis=0, concat_axis=0, tiled=True),
+        exchange_in_pairs(key_pages, "dp", 0, 0),
         lax.all_to_all(value_pages, "dp", split_axis=0, concat_axis=0, tiled=True),
     )
     kv_width = KV_HEADS * HEAD_DIM

time: 267 us -> 268 us (level)
  starting transfers between devices: 8.76 us -> 13.6 us
  waiting for transfers between devices: 82.2 us -> 79 us
    ppermute x0 -> x7, starting transfers between devices: none -> 8.31 us  [exchange_in_pairs(): part = lax.ppermute(part, axis, [(d, d ^ mask) for d in range(ways)])]
    all_to_all x1, waiting for transfers between devices: 6.55 us -> 0.01 us  [body(): lax.all_to_all(value_pages, 'dp', split_axis=0, concat_axis=0, tiled=True)]
    ppermute x0 -> x7, waiting for transfers between devices: none -> 6.41 us  [exchange_in_pairs(): part = lax.ppermute(part, axis, [(d, d ^ mask) for d in range(ways)])]
    all_to_all x1 -> x0, waiting for transfers between devices: 3.87 us -> none  [body(): lax.all_to_all(key_pages, 'dp', split_axis=0, concat_axis=0, tiled=True)]
    all_to_all x1 -> x0, starting transfers between devices: 3.5 us -> none  [body(): lax.all_to_all(key_pages, 'dp', split_axis=0, concat_axis=0, tiled=True)]
  transfers between devices with their start and end apart: 4 -> 10, of which waited for: 4 -> 4; matrix products, arithmetic and copies ran while one was open for 15% -> 15% of each run, Pallas kernels for 0% -> 0%
where the time goes in v1:
time: 268 us; the launch traced here: 265 us
  matrix products  93.5 us (35%)
  waiting for transfers between devices  79 us (29%)
  local copies, waits for them, and re-layouts  29.1 us (11%)
  blocking collectives  24 us (9%)
  between operations  14.9 us (6%)
  starting transfers between devices  13.6 us (5%)
  other arithmetic  10.6 us (4%)
    reduce_scatter x1, waiting for transfers between devices, moe_finish(): lax.psum_scatter(row_terms.reshape((n_dp, n_ex) + row_terms.shape[1:]), '...  59.4 us
    all_to_all x1, blocking collectives, moe_finish(): lax.all_to_all(row_terms, 'expert', split_axis=0, concat_axis=0, tiled=True)  24 us
    dot_general x1, matrix products, moe_finish(): jnp.einsum('tbxmf,xfd->tbxmd', hidden_act, w_down, preferred_element_type...  23.1 us
    dot_general x1, matrix products, moe_finish(): jnp.einsum('tbrxm,tbxmd->btrd', weights, partial, preferred_element_type=...  20.2 us
    dot_general x1, matrix products, moe_finish(): jnp.einsum('tbxmd,xdf->tbxmf', slots, w_gate, preferred_element_type=jnp....  13.9 us
    dot_general x1, matrix products, moe_finish(): jnp.einsum('tbxmd,xdf->tbxmf', slots, w_up, preferred_element_type=jnp.fl...  13.7 us
    all_gather x1, waiting for transfers between devices, moe_layer(): gathered = lax.all_gather(payload, ('dp', 'expert'), axis=1, tiled=False)  13.1 us
    dot_general x1, matrix products, moe_finish(): jnp.einsum('tbrxm,tbrd->tbxmd', sender.astype(jnp.bfloat16), all_rows, pr...  10.5 us
  transfers between devices with their start and end apart: 10, of which 4 were waited for; matrix products, arithmetic and copies ran while one was open for 15% of the time, Pallas kernels for 0%

profile of v1, /device:TPU:0, one launch (start us, length us, event | category | flops | bytes accessed | tf_op | source)
XLA Modules:
  0.0 264.5 jit_solution(14188691641126004756)
XLA Ops:
  8.0 0.8 copy.104
  8.7 1.0 fusion.53
  10.2 1.0 fusion.55
  11.5 1.5 gather_fusion.1
  13.5 0.8 concatenate.3
  14.3 5.2 %all-to-all-start = ((bf16[8,4,16,512]{3,2,1,0:T(8,128)(2,1)}), bf16[8,4,16,512]{3,2,1,0:T(8,128)(2,1)S(1)}, u32[]{:S(2)}, u32[]{:S(2)}) async-start(bf16[8,4,16,512]{3,2,1,0:T(8,128)(2,1)} %param.27), calls=%async_computation | async-start | bytes 1048576 | tf_op jit(solution)/shard_map/all_to_all | solution.py:196
  19.7 2.7 %collective-permute-start.6 = (bf16[1,4,16,512]{3,2,1,0:T(8,128)(2,1)S(1)}, bf16[1,4,16,512]{3,2,1,0:T(8,128)(2,1)S(1)}, u32[]{:S(2)}, u32[]{:S(2)}) collective-permute-start(bf16[1,4,16,512]{3,2,1,0:T(8,128)(2,1)S(1)} %get-tuple-element.13), channel_id=1, source_target_pairs={{0,28},{4,24},{8,20},{12,16},{16,12},{20,8},{24,4},{28,0},{1,29},{... | collective-permute-start | bytes 196616 | tf_op jit(solution)/shard_map/ppermute | solution.py:26
  22.8 1.5 collective-permute-start.3
  27.3 2.0 gather_fusion
  29.4 3.2 %fusion.68 = (f32[2,16,8,8]{3,0,2,1:T(2,128)S(1)}, f32[2,16,8,8,2]{3,4,0,2,1:T(2,128)}) fusion(bf16[2,16,8,8,64]{4,3,2,1,0:T(8,128)(2,1)S(1)} %reshape.268, bf16[2,16,8,64,1]{3,2,1,0,4:T(8,128)(2,1)S(1)} %bitcast.102, pred[2,2]{1,0:T(4,128)(4,1)S(1)} %iota_compare_fusion.3), kind=kOutput, calls=%fused_computation.116 | convolution fusion | flops 534528 | bytes 319492 | tf_op jit(solution)/shard_map/trkgh,urkh->trkgu/dot_general | solution.py:62
  32.6 1.5 collective-permute-start.1
  34.2 2.8 %collective-permute-done.1 = bf16[1,4,16,512]{3,2,1,0:T(8,128)(2,1)S(1)} collective-permute-done((bf16[1,4,16,512]{3,2,1,0:T(8,128)(2,1)S(1)}, bf16[1,4,16,512]{3,2,1,0:T(8,128)(2,1)S(1)}, u32[]{:S(2)}, u32[]{:S(2)}) %collective-permute-start.1) | collective-permute-done | bytes 65568 | tf_op jit(solution)/shard_map/ppermute | solution.py:26
  37.0 1.5 collective-permute-start.5
  38.5 3.6 %collective-permute-done.5 = bf16[1,4,16,512]{3,2,1,0:T(8,128)(2,1)S(1)} collective-permute-done((bf16[1,4,16,512]{3,2,1,0:T(8,128)(2,1)S(1)}, bf16[1,4,16,512]{3,2,1,0:T(8,128)(2,1)S(1)}, u32[]{:S(2)}, u32[]{:S(2)}) %collective-permute-start.5) | collective-permute-done | bytes 65568 | tf_op jit(solution)/shard_map/ppermute | solution.py:26
  42.2 2.5 gather_fusion.3
  44.7 2.5 gather_fusion.2
  47.1 4.0 %broadcast_select_fusion = (bf16[160,16,512]{2,1,0:T(8,128)(2,1)}, bf16[160,16,512]{2,1,0:T(8,128)(2,1)S(1)}) fusion(bf16[160,16,512]{2,1,0:T(8,128)(2,1)} %gather_fusion.3, pred[160]{0:T(512)(128)(4,1)S(1)} %get-tuple-element.9, bf16[160,16,512]{2,1,0:T(8,128)(2,1)} %gather_fusion.2), kind=kLoop, calls=%fused_computation.23 | loop fusion | flops 2621440 | bytes 10485920 | tf_op jit(solution)/shard_map/jit(_take)/select_n | solution.py:45
  51.1 7.5 %reshape.267 = bf16[16,160,8,64]{3,2,1,0:T(8,128)(2,1)} reshape(bf16[160,16,512]{2,1,0:T(8,128)(2,1)} %get-tuple-element.23) | data formatting | bytes 5242880 | tf_op jit(solution)/shard_map/reshape | solution.py:45
  58.6 4.6 %reshape.265 = bf16[16,160,8,64]{3,2,1,0:T(8,128)(2,1)} reshape(bf16[160,16,512]{2,1,0:T(8,128)(2,1)S(1)} %get-tuple-element.24) | data formatting | bytes 5242880 | tf_op jit(solution)/shard_map/reshape | solution.py:48
  63.2 6.5 %bitcast_reduce_fusion = (f32[2,16,8,8]{3,0,2,1:T(2,128)S(1)}, f32[16,8,160,2,8]{2,4,3,1,0:T(8,128)S(1)}) fusion(pred[16,160]{1,0:T(8,128)(4,1)S(1)} %iota_compare_fusion.1, bf16[2,16,8,8,64]{4,3,2,1,0:T(8,128)(2,1)S(1)} %reshape.268, bf16[16,160,8,64,1]{3,2,1,0,4:T(8,128)(2,1)} %bitcast.99), kind=kOutput, calls=%fused_computation.26 | convolution fusion | flops 42924032 | bytes 4205056 | tf_op jit(solution)/shard_map/trkgh,rlkh->trkgl/dot_general | solution.py:57
  70.3 1.0 fusion.25
  71.4 1.5 fusion.27
  73.7 1.2 convert_element_type.77
  74.9 13.1 %all-gather.3.cloned.1.call-done = bf16[2,512,2944]{2,1,0:T(8,128)(2,1)} async-done(((bf16[2,16,2944]{2,1,0:T(8,128)(2,1)}), bf16[2,512,2944]{2,1,0:T(8,128)(2,1)}) %all-gather.3.cloned.1.call-update) | async-done | bytes 6029328 | tf_op jit(solution)/shard_map/all_gather | solution.py:107
  88.0 1.1 slice.25
  91.7 10.5 %convolution_convert_fusion = bf16[2,32,16,2,2880]{4,2,3,1,0:T(8,128)(2,1)} fusion(bf16[2,32,16,2944]{3,2,1,0:T(8,128)(2,1)} %bitcast.93, s32[2,32,16,16]{3,2,0,1:T(8,128)S(1)} %copy.125, pred[2,32,16,16]{3,2,0,1:T(8,128)(4,1)S(1)} %copy.124), kind=kOutput, calls=%fused_computation.16 | convolution fusion | flops 194707456 | bytes 17907712 | tf_op jit(solution)/shard_map/tbrxm,tbrd->tbxmd/dot_general | solution.py:127
  102.3 13.7 %fusion.4 = f32[16,2,32,2,256]{4,2,3,1,0:T(8,128)S(1)} fusion(bf16[16,2880,256]{2,1,0:T(8,128)(2,1)} %param.21, bf16[2,32,16,2,2880]{4,2,3,1,0:T(8,128)(2,1)} %convolution_convert_fusion), kind=kOutput, calls=%fused_computation.8 | convolution fusion | flops 3019898880 | bytes 37486592 | tf_op jit(solution)/shard_map/tbxmd,xdf->tbxmf/dot_general | solution.py:134
  116.0 13.9 %fusion.32 = bf16[2,32,16,2,256]{4,1,3,0,2:T(8,128)(2,1)S(1)} fusion(bf16[16,2880,256]{2,1,0:T(8,128)(2,1)} %param.20, bf16[2,32,16,2,2880]{4,2,3,1,0:T(8,128)(2,1)} %convolution_convert_fusion, f32[16,2,32,2,256]{4,2,3,1,0:T(8,128)S(1)} %fusion.4), kind=kOutput, calls=%fused_computation.37 | convolution fusion | flops 3024093184 | bytes 38535168 | tf_op jit(solution)/shard_map/tbxmd,xdf->tbxmf/dot_general | solution.py:133
  129.9 23.1 %convert_bitcast_fusion = bf16[2,32,16,2,2880]{4,1,3,0,2:T(8,128)(2,1)} fusion(bf16[2,32,16,2,256]{4,1,3,0,2:T(8,128)(2,1)S(1)} %fusion.32, bf16[16,256,2880]{1,2,0:T(8,128)(2,1)} %param.22), kind=kOutput, calls=%fused_computation.13 | convolution fusion | flops 3025797120 | bytes 36438016 | tf_op jit(solution)/shard_map/tbxmf,xfd->tbxmd/dot_general | solution.py:138
  153.0 20.2 %bitcast_convert_fusion = bf16[32,2,16,2880]{3,2,1,0:T(8,128)(2,1)} fusion(bf16[2,32,16,2,2880]{4,1,3,0,2:T(8,128)(2,1)} %convert_bitcast_fusion, bf16[2,32,16,16]{3,2,0,1:T(8,128)(2,1)S(1)} %copy.127, s32[2,32,16,16]{3,2,0,1:T(8,128)S(1)} %copy.125, pred[2,32,16,16]{3,2,0,1:T(8,128)(4,1)S(1)} %copy.124), kind=kOutput, calls=%fused_computation.10 | convolution fusion | flops 191791104 | bytes 17809408 | tf_op jit(solution)/shard_map/tbrxm,tbxmd->btrd/dot_general | solution.py:162
  173.2 59.4 %reduce-scatter.2.cloned.1.call-done = bf16[1,4,2,16,2880]{4,3,2,1,0:T(8,128)(2,1)} async-done(((bf16[8,4,2,16,2880]{4,3,2,1,0:T(8,128)(2,1)}), bf16[1,4,2,16,2880]{4,3,2,1,0:T(8,128)(2,1)}) %reduce-scatter.2.cloned.1.call-update) | async-done | bytes 737296 | tf_op jit(solution)/shard_map/reduce_scatter | solution.py:165
  232.7 24.0 %all_to_all.10 = bf16[4,2,16,2880]{3,2,1,0:T(8,128)(2,1)S(1)} all-to-all(bf16[4,2,16,2880]{3,2,1,0:T(8,128)(2,1)} %bitcast.100), channel_id=1, replica_groups=mesh['dp'=8,'expert'=4] {'expert'}, dimensions={0} | all-to-all | bytes 1474560 | tf_op jit(solution)/shard_map/all_to_all | solution.py:171
  (105 shorter events, 10.3 us)
Async XLA Ops:
  7.2 4.1 %copy-start = (bf16[2880,64]{0,1:T(8,128)(2,1)S(1)}, bf16[2880,64]{0,1:T(8,128)(2,1)}, u32[]{:S(2)}) copy-start(bf16[2880,64]{0,1:T(8,128)(2,1)} %param.18) | copy-start | bytes 1105924
  7.2 80.8 %all-gather.3.cloned.1.call-start = ((), (), s32[]{:S(2)}) async-start(), calls=%async_computation.4 | async-start | bytes 6217728 | tf_op jit(solution)/shard_map/all_gather | solution.py:107
  13.0 6.6 %copy-start.4 = (bf16[8,4,16,512]{3,2,1,0:T(8,128)(2,1)S(1)}, bf16[8,4,16,512]{3,2,1,0:T(8,128)(2,1)}, u32[]{:S(2)}) copy-start(bf16[8,4,16,512]{3,2,1,0:T(8,128)(2,1)} %param.26) | copy-start | bytes 1572868
  13.0 12.0 %copy-start.10 = (s32[1,16]{1,0:T(1,128)S(1)}, s32[1,16]{1,0:T(1,128)}, u32[]{:S(2)}) copy-start(s32[1,16]{1,0:T(1,128)} %param.28) | copy-start | bytes 196
  13.1 12.8 %copy-start.8 = (bf16[2,16,512]{2,1,0:T(8,128)(2,1)S(1)}, bf16[2,16,512]{2,1,0:T(8,128)(2,1)}, u32[]{:S(2)}) copy-start(bf16[2,16,512]{2,1,0:T(8,128)(2,1)} %param.24) | copy-start | bytes 98308
  13.1 12.9 %copy-start.9 = (bf16[2,16,512]{2,1,0:T(8,128)(2,1)S(1)}, bf16[2,16,512]{2,1,0:T(8,128)(2,1)}, u32[]{:S(2)}) copy-start(bf16[2,16,512]{2,1,0:T(8,128)(2,1)} %param.25) | copy-start | bytes 98308
  13.1 13.6 %copy-start.5 = (bf16[2,16,4096]{2,1,0:T(8,128)(2,1)S(1)}, bf16[2,16,4096]{2,1,0:T(8,128)(2,1)}, u32[]{:S(2)}) copy-start(bf16[2,16,4096]{2,1,0:T(8,128)(2,1)} %param.23) | copy-start | bytes 786436
  13.1 14.2 %copy-start.2 = (s32[1,32]{1,0:T(1,128)S(1)}, s32[1,32]{1,0:T(1,128)}, u32[]{:S(2)}) copy-start(s32[1,32]{1,0:T(1,128)} %param.29) | copy-start | bytes 388
  14.3 30.4 %all-to-all-start = ((bf16[8,4,16,512]{3,2,1,0:T(8,128)(2,1)}), bf16[8,4,16,512]{3,2,1,0:T(8,128)(2,1)S(1)}, u32[]{:S(2)}, u32[]{:S(2)}) async-start(bf16[8,4,16,512]{3,2,1,0:T(8,128)(2,1)} %param.27), calls=%async_computation | async-start | bytes 1048576 | tf_op jit(solution)/shard_map/all_to_all | solution.py:196
  19.4 213.2 %reduce-scatter.2.cloned.1.call-start = ((), (), s32[]{:S(2)}) async-start(), calls=%async_computation.3 | async-start | bytes 6782976 | tf_op jit(solution)/shard_map/reduce_scatter | solution.py:165
  19.7 22.5 %collective-permute-start.6 = (bf16[1,4,16,512]{3,2,1,0:T(8,128)(2,1)S(1)}, bf16[1,4,16,512]{3,2,1,0:T(8,128)(2,1)S(1)}, u32[]{:S(2)}, u32[]{:S(2)}) collective-permute-start(bf16[1,4,16,512]{3,2,1,0:T(8,128)(2,1)S(1)} %get-tuple-element.13), channel_id=1, source_target_pairs={{0,28},{4,24},{8,20},{12,16},{16,12},{20,8},{24,4},{28,0},{1,29},{... | collective-permute-start | bytes 196616 | tf_op jit(solution)/shard_map/ppermute | solution.py:26
  22.3 16.2 %collective-permute-start.4 = (bf16[1,4,16,512]{3,2,1,0:T(8,128)(2,1)S(1)}, bf16[1,4,16,512]{3,2,1,0:T(8,128)(2,1)S(1)}, u32[]{:S(2)}, u32[]{:S(2)}) collective-permute-start(bf16[1,4,16,512]{3,2,1,0:T(8,128)(2,1)S(1)} %get-tuple-element.14), channel_id=1, source_target_pairs={{0,20},{4,16},{8,28},{12,24},{16,4},{20,0},{24,12},{28,8},{1,21},{... | collective-permute-start | bytes 196616 | tf_op jit(solution)/shard_map/ppermute | solution.py:26
  22.8 15.6 %collective-permute-start.3 = (bf16[1,4,16,512]{3,2,1,0:T(8,128)(2,1)S(1)}, bf16[1,4,16,512]{3,2,1,0:T(8,128)(2,1)S(1)}, u32[]{:S(2)}, u32[]{:S(2)}) collective-permute-start(bf16[1,4,16,512]{3,2,1,0:T(8,128)(2,1)S(1)} %get-tuple-element.15), channel_id=1, source_target_pairs={{0,16},{4,20},{8,24},{12,28},{16,0},{20,4},{24,8},{28,12},{1,17},{... | collective-permute-start | bytes 196616 | tf_op jit(solution)/shard_map/ppermute | solution.py:26
  24.3 14.1 %collective-permute-start.2 = (bf16[1,4,16,512]{3,2,1,0:T(8,128)(2,1)S(1)}, bf16[1,4,16,512]{3,2,1,0:T(8,128)(2,1)S(1)}, u32[]{:S(2)}, u32[]{:S(2)}) collective-permute-start(bf16[1,4,16,512]{3,2,1,0:T(8,128)(2,1)S(1)} %get-tuple-element.16), channel_id=1, source_target_pairs={{0,12},{4,8},{8,4},{12,0},{16,28},{20,24},{24,20},{28,16},{1,13},{... | collective-permute-start | bytes 196616 | tf_op jit(solution)/shard_map/ppermute | solution.py:26
  24.4 8.3 %collective-permute-start = (bf16[1,4,16,512]{3,2,1,0:T(8,128)(2,1)S(1)}, bf16[1,4,16,512]{3,2,1,0:T(8,128)(2,1)S(1)}, u32[]{:S(2)}, u32[]{:S(2)}) collective-permute-start(bf16[1,4,16,512]{3,2,1,0:T(8,128)(2,1)S(1)} %get-tuple-element.18), channel_id=1, source_target_pairs={{0,4},{4,0},{8,12},{12,8},{16,20},{20,16},{24,28},{28,24},{1,5},{5... | collective-permute-start | bytes 196616 | tf_op jit(solution)/shard_map/ppermute | solution.py:26
  32.6 4.3 %collective-permute-start.1 = (bf16[1,4,16,512]{3,2,1,0:T(8,128)(2,1)S(1)}, bf16[1,4,16,512]{3,2,1,0:T(8,128)(2,1)S(1)}, u32[]{:S(2)}, u32[]{:S(2)}) collective-permute-start(bf16[1,4,16,512]{3,2,1,0:T(8,128)(2,1)S(1)} %get-tuple-element.17), channel_id=1, source_target_pairs={{0,8},{4,12},{8,0},{12,4},{16,24},{20,28},{24,16},{28,20},{1,9},{5... | collective-permute-start | bytes 196616 | tf_op jit(solution)/shard_map/ppermute | solution.py:26
  37.0 5.2 %collective-permute-start.5 = (bf16[1,4,16,512]{3,2,1,0:T(8,128)(2,1)S(1)}, bf16[1,4,16,512]{3,2,1,0:T(8,128)(2,1)S(1)}, u32[]{:S(2)}, u32[]{:S(2)}) collective-permute-start(bf16[1,4,16,512]{3,2,1,0:T(8,128)(2,1)S(1)} %get-tuple-element.20), channel_id=1, source_target_pairs={{0,24},{4,28},{8,16},{12,20},{16,8},{20,12},{24,0},{28,4},{1,25},{... | collective-permute-start | bytes 196616 | tf_op jit(solution)/shard_map/ppermute | solution.py:26
  63.2 8.2 %slice-start = ((s8[5242880]{0:T(1024)(128)(4,1)}), s8[4194304]{0:T(1024)(128)(4,1)S(1)}, s32[]{:S(2)}) async-start(s8[5242880]{0:T(1024)(128)(4,1)} %bitcast.96), calls=%async_computation.5 | async-start | bytes 8388608
  63.2 6.6 %copy-start.6 = (f32[2,16,8,8,2]{3,4,0,2,1:T(2,128)S(1)}, f32[2,16,8,8,2]{3,4,0,2,1:T(2,128)}, u32[]{:S(2)}) copy-start(f32[2,16,8,8,2]{3,4,0,2,1:T(2,128)} %get-tuple-element.28) | copy-start | bytes 49156
  63.2 8.2 %slice-start.1 = ((s8[5242880]{0:T(1024)(128)(4,1)}), s8[1048576]{0:T(1024)(128)(4,1)S(1)}, s32[]{:S(2)}) async-start(s8[5242880]{0:T(1024)(128)(4,1)} %bitcast.96), calls=%async_computation.6 | async-start | bytes 2097152
  71.4 1.5 copy-start.7
  173.2 83.5 %copy-start.3 = (bf16[2,16,2880]{2,1,0:T(8,128)(2,1)S(1)}, bf16[2,16,2880]{2,1,0:T(8,128)(2,1)}, u32[]{:S(2)}) copy-start(bf16[2,16,2880]{2,1,0:T(8,128)(2,1)} %param.16) | copy-start | bytes 552964
  173.2 84.2 %copy-start.1 = (bf16[2880,64]{0,1:T(8,128)(2,1)S(1)}, bf16[2880,64]{0,1:T(8,128)(2,1)}, u32[]{:S(2)}) copy-start(bf16[2880,64]{0,1:T(8,128)(2,1)} %param.18) | copy-start | bytes 1105924
Sparse Core Ops, SparseCore 0:
  14.4 73.6 all-gather.2
  173.3 59.2 reduce-scatter.1
